TPU v7x, 128 devices: a whole 4x4x4 slice. The times are simulated.
128 devices in a mesh: ra: 16 (over z, y), dec: 8 (over x, core).
Axes of the slice: x: 4, y: 4, z: 4, core: 2. Of those that a mesh axis runs over, the one named last changes fastest.
Arguments:
- features: bfloat16 [512, 256, 128], P('ra', 'dec'), may hold values from -6 to 6
- conv_weight: bfloat16 [3, 3, 128, 128], replicated, may hold values from -0.1875 to 0.1875
- conv_bias: float32 [128], replicated, may hold values from -3 to 3
- corners: int32 [16, 8, 200, 2], P('ra', 'dec'), may hold values from 0 to 25
- owner_ids: int32 [16, 8, 200, 1], P('ra', 'dec'), may hold values from 0 to 127; in each aligned block of 200 rows (0 to 199, 200 to 399, ..., all dimensions but the last counted through in order) at most 3 rows name the same one
- labels: int32 [16, 8, 200], P('ra', 'dec'), may hold values from 0 to 2
- head_w1: bfloat16 [128, 6272, 512], P(('ra', 'dec')), may hold values from -0.078125 to 0.078125
- head_b1: float32 [128, 512], P(('ra', 'dec')), may hold values from -3 to 3
- head_w2: bfloat16 [128, 512, 3], P(('ra', 'dec')), may hold values from -1 to 1
- head_b2: float32 [128, 3], P(('ra', 'dec')), may hold values from -4 to 4
Outputs:
- grad_features: bfloat16 [512, 256, 128], P('ra', 'dec')
- grad_conv: float32 [3, 3, 128, 128], replicated
- grad_w1: bfloat16 [128, 6272, 512], P(('ra', 'dec'))
Inputs may be any that keep to these rules, and one draw needn't show every extreme that they name: `corners`: every crop lies inside its own tile. `owner_ids`: at most 3 objects of one tile go to one expert, and every expert gets some object.
All inputs are finite; a program needn't handle non-finite values.
Results may differ from a plain program's by a relative error of at most 0.0095.
Values may be sent and summed in bfloat16 or wider, within the bound.
No kernel may reach another device: no remote copies, remote signals or barrier semaphores. Data moves between devices by JAX's collectives and lax.ppermute only.
A program may use at most 128 MiB of HBM per device.

v0:
```python
import jax
import jax.numpy as jnp
from jax import lax
from jax.sharding import PartitionSpec as P

CROP = 7
loss_scale = 8.0


def padded_2(cells, sides, width):
    for axis, dim in sides:
        count = lax.axis_size(axis)
        ends = count - 1
        head = lax.slice_in_dim(cells, 0, width, axis=dim)
        tail = lax.slice_in_dim(cells, cells.shape[dim] - width, cells.shape[dim], axis=dim)
        cells = jnp.concatenate(
            [
                lax.ppermute(tail, axis, [(i, (i + 1) % count) for i in range(ends)]),
                cells,
                lax.ppermute(head, axis, [((i + 1) % count, i) for i in range(ends)]),
            ],
            axis=dim,
        )
    return cells


def silu_slope(value):
    logistic = jax.nn.sigmoid(value)
    return logistic * (1.0 + value * (1.0 - logistic))


def rank_in_owner(owner_list, owners_all):
    onehot = (owner_list[:, None] == jnp.arange(owners_all, dtype=jnp.int32)[None, :]).astype(
        jnp.int32
    )
    running = jnp.cumsum(onehot, axis=0)
    return jnp.sum(running * onehot, axis=1) - 1


def head_pass(crop_rows, target_rows, weight_one, bias_one, weight_two, bias_two):
    hid_pre = jnp.dot(crop_rows, weight_one, preferred_element_type=jnp.float32) + bias_one[None, :]
    hidden = jax.nn.silu(hid_pre).astype(jnp.bfloat16)
    logits = jnp.dot(hidden, weight_two, preferred_element_type=jnp.float32) + bias_two[None, :]
    target = target_rows.astype(jnp.float32)
    live_float = jnp.sum(target, axis=1, keepdims=True)
    dlogit = (loss_scale * (live_float * jax.nn.sigmoid(logits) - target)).astype(jnp.bfloat16)
    hid_grad = lax.dot_general(
        dlogit, weight_two, (((1,), (1,)), ((), ())), preferred_element_type=jnp.float32
    )
    hid_grad = (hid_grad * silu_slope(hid_pre)).astype(jnp.bfloat16)
    grad_one = lax.dot_general(
        crop_rows, hid_grad, (((0,), (0,)), ((), ())), preferred_element_type=jnp.float32
    )
    crop_grad = lax.dot_general(
        hid_grad, weight_one, (((1,), (1,)), ((), ())), preferred_element_type=jnp.float32
    )
    return (grad_one.astype(jnp.bfloat16), crop_grad.astype(jnp.bfloat16))


def local(
    features, conv_weight, conv_bias, corners, owner_ids, labels, head_w1, head_b1, head_w2, head_b2
):
    tile_rows, tile_cols, channels = features.shape
    padded = padded_2(features, (("ra", 0), ("dec", 1)), 1)
    pre_conv = jnp.zeros((tile_rows * tile_cols, channels), jnp.float32)
    for row_off in range(3):
        for col_off in range(3):
            window = padded[row_off : row_off + tile_rows, col_off : col_off + tile_cols].reshape(
                -1, channels
            )
            pre_conv = pre_conv + jnp.dot(
                window, conv_weight[row_off, col_off], preferred_element_type=jnp.float32
            )
    pre_conv = (pre_conv + conv_bias[None, :]).reshape(tile_rows, tile_cols, channels)
    activation = jax.nn.silu(pre_conv).astype(jnp.bfloat16)
    count_ra = lax.axis_size("ra")
    count_dec = lax.axis_size("dec")
    owners_all = count_ra * count_dec
    owner_list = owner_ids.reshape(-1)
    corner_list = corners.reshape(-1, 2)
    object_count = owner_list.shape[0]
    capacity = (object_count + owners_all - 1) // owners_all + 1
    slot_total = owners_all * capacity
    classes = head_w2.shape[2]
    crop_size = CROP * CROP * channels
    slot_rank = rank_in_owner(owner_list, owners_all)
    slot_index = owner_list * capacity + slot_rank
    offsets = jnp.arange(CROP, dtype=jnp.int32)
    row_index = corner_list[:, 0][:, None, None] + offsets[None, :, None]
    col_index = corner_list[:, 1][:, None, None] + offsets[None, None, :]
    crop_rows = activation[row_index, col_index].reshape(object_count, crop_size)
    onehot_label = (
        labels.reshape(-1)[:, None] == jnp.arange(classes, dtype=jnp.int32)[None, :]
    ).astype(jnp.bfloat16)
    slot_object = (
        jnp.full((slot_total,), -1, jnp.int32)
        .at[slot_index]
        .set(jnp.arange(object_count, dtype=jnp.int32))
    )
    slot_live = slot_object >= 0
    slot_safe = jnp.where(slot_live, slot_object, 0)
    send_rows = jnp.where(
        slot_live[:, None], jnp.take(crop_rows, slot_safe, axis=0), jnp.zeros((), jnp.bfloat16)
    )
    send_target = jnp.where(
        slot_live[:, None], jnp.take(onehot_label, slot_safe, axis=0), jnp.zeros((), jnp.bfloat16)
    )
    weight_one = head_w1[0]
    bias_one = head_b1[0]
    weight_two = head_w2[0]
    bias_two = head_b2[0]
    got_rows, got_target = (
        lax.all_to_all(
            send_rows.reshape(owners_all, capacity, crop_size),
            ("ra", "dec"),
            split_axis=0,
            concat_axis=0,
            tiled=True,
        ),
        lax.all_to_all(
            send_target.reshape(owners_all, capacity, classes),
            ("ra", "dec"),
            split_axis=0,
            concat_axis=0,
            tiled=True,
        ),
    )
    grad_one, crop_grad = head_pass(
        got_rows.reshape(-1, crop_size),
        got_target.reshape(-1, classes),
        weight_one,
        bias_one,
        weight_two,
        bias_two,
    )
    returned = lax.all_to_all(
        crop_grad.reshape(owners_all, capacity, crop_size),
        ("ra", "dec"),
        split_axis=0,
        concat_axis=0,
        tiled=True,
    )
    back_rows = jnp.take(returned.reshape(-1, crop_size), slot_index, axis=0)
    values = back_rows.reshape(object_count, CROP, CROP, channels).astype(jnp.float32)
    act_grad = (
        jnp.zeros((tile_rows, tile_cols, channels), jnp.float32)
        .at[row_index, col_index]
        .add(values)
    )
    pre_grad = (act_grad * silu_slope(pre_conv)).astype(jnp.bfloat16)
    grad_padded = padded_2(pre_grad, (("ra", 0), ("dec", 1)), 1)
    pre_flat = pre_grad.reshape(-1, channels)
    tap_list = []
    grad_feat = jnp.zeros((tile_rows * tile_cols, channels), jnp.float32)
    for row_off in range(3):
        for col_off in range(3):
            window = padded[row_off : row_off + tile_rows, col_off : col_off + tile_cols].reshape(
                -1, channels
            )
            tap_list.append(
                lax.dot_general(
                    window, pre_flat, (((0,), (0,)), ((), ())), preferred_element_type=jnp.float32
                )
            )
            shifted = grad_padded[
                2 - row_off : 2 - row_off + tile_rows, 2 - col_off : 2 - col_off + tile_cols
            ].reshape(-1, channels)
            grad_feat = grad_feat + lax.dot_general(
                shifted,
                conv_weight[row_off, col_off],
                (((1,), (1,)), ((), ())),
                preferred_element_type=jnp.float32,
            )
    local_taps = jnp.stack(tap_list).reshape(3, 3, channels, channels)
    grad_conv = lax.psum(local_taps, ("ra", "dec"))
    grad_features = grad_feat.reshape(tile_rows, tile_cols, channels).astype(jnp.bfloat16)
    return (grad_features, grad_conv, grad_one[None])


def solution(mesh):
    in_specs = (
        P("ra", "dec", None),
        P(),
        P(),
        P("ra", "dec", None, None),
        P("ra", "dec", None, None),
        P("ra", "dec", None),
        P(("ra", "dec"), None, None),
        P(("ra", "dec"), None),
        P(("ra", "dec"), None, None),
        P(("ra", "dec"), None),
    )
    out_specs = (P("ra", "dec", None), P(), P(("ra", "dec"), None, None))
    return jax.shard_map(local, mesh=mesh, in_specs=in_specs, out_specs=out_specs, check_vma=False)
```

profile of v0, /device:TPU:1, one launch (start us, length us, event | category | flops | bytes accessed | tf_op | source)
XLA Modules:
  0.0 652.4 jit_solution(923496613759407383)
XLA Ops:
  7.2 0.8 iota_compare_fusion.1
  8.3 0.9 fusion.48
  9.1 0.7 compare_select_fusion.2
  9.8 1.2 scatter_custom_fusion
  11.1 0.8 fusion.49
  11.9 1.4 gather_fusion
  13.4 0.3 gather.22
  13.9 0.2 broadcast_in_dim.101
  14.2 0.7 copy.30
  14.9 11.5 %all-to-all-start = ((bf16[128,3,3]{1,2,0:T(4,128)(2,1)}), bf16[128,3,3]{1,2,0:T(4,128)(2,1)S(1)}, u32[]{:S(2)}, u32[]{:S(2)}) async-start(bf16[128,3,3]{1,2,0:T(4,128)(2,1)} %copy.30), calls=%async_computation | async-start | bytes 262144 | tf_op jit(solution)/shard_map/all_to_all | solution.py:120
  26.4 0.7 fusion.106
  27.2 3.3 collective-permute-start
  30.4 1.3 collective-permute-start.1
  31.7 0.8 fusion.107
  32.8 0.3 broadcast_or_fusion
  33.1 0.4 reshape.291
  33.5 1.1 constant_dynamic-update-slice_fusion.3
  34.7 0.5 collective-permute-done.1
  35.2 4.5 collective-permute-start.2
  39.7 2.1 collective-permute-start.3
  42.3 2.4 collective-permute-done.3
  44.7 0.3 pad_maximum_fusion.4
  46.9 107.8 %gather_fusion.1 = bf16[9800,128]{1,0:T(8,128)(2,1)} fusion(bf16[32,32,128]{2,1,0:T(8,128)(2,1)S(1)} %multiply_convert_fusion.4, s32[9800]{0:T(1024)S(1)} %reshape.291), kind=kCustom, calls=%fused_computation.1 | custom fusion | bytes 5096000 | tf_op jit(solution)/shard_map/gather | solution.py:91
  154.6 4.5 reshape.263
  159.2 5.8 gather_fusion.2
  165.0 11.5 %gather.25 = bf16[128,3,6272]{2,1,0:T(4,128)(2,1)} reshape(bf16[384,6272]{1,0:T(8,128)(2,1)} %gather_fusion.2) | data formatting | bytes 9633792 | tf_op jit(solution)/shard_map/jit(_take)/gather | solution.py:103
  176.4 9.0 %select_select_fusion = bf16[128,3,6272]{2,1,0:T(4,128)(2,1)} fusion(bf16[128,3,6272]{2,1,0:T(4,128)(2,1)} %gather.25, pred[128,3]{1,0:T(8,128)(4,1)S(1)} %broadcast_in_dim.103, pred[128,3]{1,0:T(8,128)(4,1)S(1)} %broadcast_in_dim.101), kind=kLoop, calls=%fused_computation.12 | loop fusion | flops 4816896 | bytes 9634560 | tf_op jit(solution)/shard_map/jit(_where)/select_n | solution.py:102
  185.4 11.1 %all-to-all-start.1 = ((bf16[128,3,6272]{2,1,0:T(4,128)(2,1)}), bf16[128,3,6272]{2,1,0:T(4,128)(2,1)}, u32[]{:S(2)}, u32[]{:S(2)}) async-start(bf16[128,3,6272]{2,1,0:T(4,128)(2,1)} %select_select_fusion), calls=%async_computation.1 | async-start | bytes 12845056 | tf_op jit(solution)/shard_map/all_to_all | solution.py:113
  197.2 76.0 %all-to-all-done.1 = bf16[128,3,6272]{2,1,0:T(4,128)(2,1)} async-done(((bf16[128,3,6272]{2,1,0:T(4,128)(2,1)}), bf16[128,3,6272]{2,1,0:T(4,128)(2,1)}, u32[]{:S(2)}, u32[]{:S(2)}) %all-to-all-start.1) | async-done | bytes 4816928 | tf_op jit(solution)/shard_map/all_to_all | solution.py:113
  273.2 12.4 %reshape.264 = bf16[384,6272]{1,0:T(8,128)(2,1)} reshape(bf16[128,3,6272]{2,1,0:T(4,128)(2,1)} %all-to-all-done.1) | data formatting | bytes 9633792 | tf_op jit(solution)/shard_map/reshape | solution.py:129
  285.6 6.3 fusion.4
  292.0 0.8 fusion.7
  292.7 8.7 %convolution_convert_fusion.1 = bf16[384,6272]{1,0:T(8,128)(2,1)} fusion(bf16[384,512]{1,0:T(8,128)(2,1)S(1)} %fusion.7, bf16[1,6272,512]{2,1,0:T(8,128)(2,1)} %param.16), kind=kOutput, calls=%fused_computation.7 | convolution fusion | flops 2468659200 | bytes 11632640 | tf_op jit(solution)/shard_map/dot_general | solution.py:54
  301.5 11.5 %reshape.265 = bf16[128,3,6272]{2,1,0:T(4,128)(2,1)} reshape(bf16[384,6272]{1,0:T(8,128)(2,1)} %convolution_convert_fusion.1) | data formatting | bytes 9633792 | tf_op jit(solution)/shard_map/reshape | solution.py:137
  313.0 6.5 %all-to-all-start.2 = ((bf16[128,3,6272]{2,1,0:T(4,128)(2,1)}), bf16[128,3,6272]{2,1,0:T(4,128)(2,1)}, u32[]{:S(2)}, u32[]{:S(2)}) async-start(bf16[128,3,6272]{2,1,0:T(4,128)(2,1)} %reshape.265), calls=%async_computation.2 | async-start | bytes 12845056 | tf_op jit(solution)/shard_map/all_to_all | solution.py:136
  319.6 0.2 and_reduce_fusion
  320.1 0.4 copy.26
  320.5 0.4 reshape.321
  321.0 7.8 %fusion = bf16[1,6272,512]{2,1,0:T(8,128)(2,1)} fusion(bf16[384,6272]{1,0:T(8,128)(2,1)} %reshape.264, bf16[384,512]{1,0:T(8,128)(2,1)S(1)} %fusion.7), kind=kOutput, calls=%fused_computation.8 | convolution fusion | flops 2469462016 | bytes 11632640 | tf_op jit(solution)/shard_map/dot_general | solution.py:51
  328.8 67.3 %all-to-all-done.2 = bf16[128,3,6272]{2,1,0:T(4,128)(2,1)} async-done(((bf16[128,3,6272]{2,1,0:T(4,128)(2,1)}), bf16[128,3,6272]{2,1,0:T(4,128)(2,1)}, u32[]{:S(2)}, u32[]{:S(2)}) %all-to-all-start.2) | async-done | bytes 4816928 | tf_op jit(solution)/shard_map/all_to_all | solution.py:136
  396.1 12.4 %reshape.266 = bf16[384,6272]{1,0:T(8,128)(2,1)} reshape(bf16[128,3,6272]{2,1,0:T(4,128)(2,1)} %all-to-all-done.2) | data formatting | bytes 9633792 | tf_op jit(solution)/shard_map/reshape | solution.py:143
  408.6 8.9 %gather_fusion.3 = bf16[200,6272]{1,0:T(8,128)(2,1)} fusion(bf16[384,6272]{1,0:T(8,128)(2,1)} %reshape.266, s32[1024]{0:T(1024)S(1)} %pad_clamp_fusion), kind=kCustom, calls=%fused_computation.3 | custom fusion | bytes 5018400 | tf_op jit(solution)/shard_map/jit(_take)/gather | solution.py:143
  417.5 5.2 gather.27
  422.6 3.0 select_convert_fusion
  425.6 6.7 %reshape.323 = f32[9800,128]{1,0:T(8,128)} reshape(f32[200,7,7,128]{3,2,1,0:T(8,128)} %select_convert_fusion) | data formatting | bytes 10035200 | tf_op jit(solution)/shard_map/convert_element_type | solution.py:144
  432.3 55.8 %scatter_custom_fusion.1 = f32[1024,128]{1,0:T(8,128)S(1)} fusion(s32[9800]{0:T(1024)S(1)} %reshape.321, f32[9800,128]{1,0:T(8,128)} %reshape.323, f32[]{:T(128)} %constant.27.clone.1), kind=kCustom, calls=%fused_computation.90 | custom fusion | flops 1254400 | bytes 524800
  488.4 0.3 fusion.21
  488.6 1.3 collective-permute-start.5
  489.9 4.0 collective-permute-start.4
  493.9 1.2 fusion.14
  495.2 0.3 fusion.20
  495.5 0.3 fusion.19
  495.7 0.3 fusion.18
  496.0 0.3 fusion.17
  496.3 0.3 fusion.16
  496.6 0.3 fusion.13
  496.9 0.3 fusion.15
  497.2 0.8 copy-done.20
  498.1 3.3 collective-permute-start.6
  501.4 3.4 collective-permute-start.7
  505.1 0.6 collective-permute-done.7
  507.8 0.9 fusion.12
  508.7 135.0 %all-reduce.3.cloned.1.call-done = f32[3,3,128,128]{3,2,1,0:T(8,128)} async-done(((f32[3,3,128,128]{3,2,1,0:T(8,128)}), f32[3,3,128,128]{3,2,1,0:T(8,128)}) %all-reduce.3.cloned.1.call-update) | async-done | bytes 589840 | tf_op jit(solution)/shard_map/psum | solution.py:175
  643.7 1.9 copy.52
  (120 shorter events, 6.6 us)
Async XLA Ops:
  7.2 284.8 %copy-start = (bf16[1,512,3]{1,2,0:T(4,128)(2,1)S(1)}, bf16[1,512,3]{1,2,0:T(4,128)(2,1)}, u32[]{:S(2)}) copy-start(bf16[1,512,3]{1,2,0:T(4,128)(2,1)} %param.18) | copy-start | bytes 9220
  7.2 34.7 %copy-start.4 = (bf16[3,3,128,128]{3,2,1,0:T(8,128)(2,1)S(1)}, bf16[3,3,128,128]{3,2,1,0:T(8,128)(2,1)}, u32[]{:S(2)}) copy-start(bf16[3,3,128,128]{3,2,1,0:T(8,128)(2,1)} %param.11) | copy-start | bytes 884740
  14.9 170.5 %all-to-all-start = ((bf16[128,3,3]{1,2,0:T(4,128)(2,1)}), bf16[128,3,3]{1,2,0:T(4,128)(2,1)S(1)}, u32[]{:S(2)}, u32[]{:S(2)}) async-start(bf16[128,3,3]{1,2,0:T(4,128)(2,1)} %copy.30), calls=%async_computation | async-start | bytes 262144 | tf_op jit(solution)/shard_map/all_to_all | solution.py:120
  27.2 6.4 collective-permute-start
  30.4 4.7 collective-permute-start.1
  33.1 12.9 %copy-start.2 = (bf16[32,32,128]{2,1,0:T(8,128)(2,1)S(1)}, bf16[32,32,128]{2,1,0:T(8,128)(2,1)}, u32[]{:S(2)}) copy-start(bf16[32,32,128]{2,1,0:T(8,128)(2,1)} %param.10) | copy-start | bytes 786436
  34.7 7.6 %copy-start.21 = (bf16[33,32,128]{2,1,0:T(8,128)(2,1)}, bf16[33,32,128]{2,1,0:T(8,128)(2,1)S(1)}, u32[]{:S(2)}) copy-start(bf16[33,32,128]{2,1,0:T(8,128)(2,1)S(1)} %get-tuple-element.28) | copy-start | bytes 811012
  35.1 6.7 %copy-start.18 = (bf16[33,32,128]{2,1,0:T(8,128)(2,1)}, bf16[33,32,128]{2,1,0:T(8,128)(2,1)S(1)}, u32[]{:S(2)}) copy-start(bf16[33,32,128]{2,1,0:T(8,128)(2,1)S(1)} %get-tuple-element.35) | copy-start | bytes 811012
  35.2 7.1 %collective-permute-start.2 = (bf16[34,1,128]{2,1,0:T(2,128)(2,1)S(1)}, bf16[34,1,128]{2,1,0:T(2,128)(2,1)S(1)}, u32[]{:S(2)}, u32[]{:S(2)}) collective-permute-start(bf16[34,1,128]{2,1,0:T(2,128)(2,1)S(1)} %get-tuple-element.22), channel_id=1, source_target_pairs={{0,1},{1,2},{2,3},{3,4},{4,5},{5,6},{6,7},{8,9},{9,10},{10,11},{11... | collective-permute-start | bytes 26120 | tf_op jit(solution)/shard_map/ppermute | solution.py:18
  39.7 5.1 collective-permute-start.3
  41.8 4.7 copy-start.24
  45.1 1.2 copy-start.6
  45.1 1.6 copy-start.12
  45.1 1.6 copy-start.14
  45.1 1.6 copy-start.16
  45.1 1.8 copy-start.8
  45.1 1.8 copy-start.10
  185.4 87.7 %all-to-all-start.1 = ((bf16[128,3,6272]{2,1,0:T(4,128)(2,1)}), bf16[128,3,6272]{2,1,0:T(4,128)(2,1)}, u32[]{:S(2)}, u32[]{:S(2)}) async-start(bf16[128,3,6272]{2,1,0:T(4,128)(2,1)} %select_select_fusion), calls=%async_computation.1 | async-start | bytes 12845056 | tf_op jit(solution)/shard_map/all_to_all | solution.py:113
  196.8 88.8 %copy-start.25 = (f32[1,512]{1,0:T(1,128)S(1)}, f32[1,512]{1,0:T(1,128)}, u32[]{:S(2)}) copy-start(f32[1,512]{1,0:T(1,128)} %param.17) | copy-start | bytes 6148
  285.6 6.4 copy-start.26
  313.0 6.9 %copy-start.23 = (s32[2]{0:T(128)S(1)}, s32[2]{0:T(128)}, u32[]{:S(2)}) copy-start(s32[2]{0:T(128)} %constant.87) | copy-start | bytes 28
  313.0 8.0 %copy-start.22 = (s32[1,1,200,1]{2,3,1,0:T(1,128)S(1)}, s32[1,1,200,1]{2,3,1,0:T(1,128)}, u32[]{:S(2)}) copy-start(s32[1,1,200,1]{2,3,1,0:T(1,128)} %param.14) | copy-start | bytes 2404
  313.0 83.2 %all-to-all-start.2 = ((bf16[128,3,6272]{2,1,0:T(4,128)(2,1)}), bf16[128,3,6272]{2,1,0:T(4,128)(2,1)}, u32[]{:S(2)}, u32[]{:S(2)}) async-start(bf16[128,3,6272]{2,1,0:T(4,128)(2,1)} %reshape.265), calls=%async_computation.2 | async-start | bytes 12845056 | tf_op jit(solution)/shard_map/all_to_all | solution.py:136
  319.5 324.1 %all-reduce.3.cloned.1.call-start = ((), (), s32[]{:S(2)}) async-start(), calls=%async_computation.3 | async-start | bytes 1179648 | tf_op jit(solution)/shard_map/psum | solution.py:175
  425.6 62.7 %copy-start.15 = (bf16[32,32,128]{2,1,0:T(8,128)(2,1)S(1)}, bf16[32,32,128]{2,1,0:T(8,128)(2,1)}, u32[]{:S(2)}) copy-start(bf16[32,32,128]{2,1,0:T(8,128)(2,1)} %copy-done.14) | copy-start | bytes 786436
  425.6 69.5 %copy-start.13 = (bf16[32,32,128]{2,1,0:T(8,128)(2,1)S(1)}, bf16[32,32,128]{2,1,0:T(8,128)(2,1)}, u32[]{:S(2)}) copy-start(bf16[32,32,128]{2,1,0:T(8,128)(2,1)} %copy-done.12) | copy-start | bytes 786436
  425.6 69.8 %copy-start.11 = (bf16[32,32,128]{2,1,0:T(8,128)(2,1)S(1)}, bf16[32,32,128]{2,1,0:T(8,128)(2,1)}, u32[]{:S(2)}) copy-start(bf16[32,32,128]{2,1,0:T(8,128)(2,1)} %copy-done.10) | copy-start | bytes 786436
  425.6 70.1 %copy-start.3 = (bf16[32,32,128]{2,1,0:T(8,128)(2,1)S(1)}, bf16[32,32,128]{2,1,0:T(8,128)(2,1)}, u32[]{:S(2)}) copy-start(bf16[32,32,128]{2,1,0:T(8,128)(2,1)} %param.10) | copy-start | bytes 786436
  432.3 63.7 %copy-start.9 = (bf16[32,32,128]{2,1,0:T(8,128)(2,1)S(1)}, bf16[32,32,128]{2,1,0:T(8,128)(2,1)}, u32[]{:S(2)}) copy-start(bf16[32,32,128]{2,1,0:T(8,128)(2,1)} %copy-done.8) | copy-start | bytes 786436
  432.3 64.6 %copy-start.7 = (bf16[32,32,128]{2,1,0:T(8,128)(2,1)S(1)}, bf16[32,32,128]{2,1,0:T(8,128)(2,1)}, u32[]{:S(2)}) copy-start(bf16[32,32,128]{2,1,0:T(8,128)(2,1)} %copy-done.6) | copy-start | bytes 786436
  488.1 8.2 %copy-start.17 = (bf16[32,32,128]{2,1,0:T(8,128)(2,1)S(1)}, bf16[32,32,128]{2,1,0:T(8,128)(2,1)}, u32[]{:S(2)}) copy-start(bf16[32,32,128]{2,1,0:T(8,128)(2,1)} %copy-done.16) | copy-start | bytes 786436
  488.1 8.5 %copy-start.19 = (bf16[33,32,128]{2,1,0:T(8,128)(2,1)S(1)}, bf16[33,32,128]{2,1,0:T(8,128)(2,1)}, u32[]{:S(2)}) copy-start(bf16[33,32,128]{2,1,0:T(8,128)(2,1)} %copy-done.18) | copy-start | bytes 811012
  488.1 16.7 %copy-start.5 = (bf16[3,3,128,128]{3,2,1,0:T(8,128)(2,1)S(1)}, bf16[3,3,128,128]{3,2,1,0:T(8,128)(2,1)}, u32[]{:S(2)}) copy-start(bf16[3,3,128,128]{3,2,1,0:T(8,128)(2,1)} %param.11) | copy-start | bytes 884740
  488.6 9.4 %collective-permute-start.5 = (bf16[1,32,128]{2,1,0:T(8,128)(2,1)S(1)}, bf16[1,32,128]{2,1,0:T(8,128)(2,1)S(1)}, u32[]{:S(2)}, u32[]{:S(2)}) collective-permute-start(bf16[1,32,128]{2,1,0:T(8,128)(2,1)S(1)} %get-tuple-element.27), channel_id=1, source_target_pairs={{8,0},{16,8},{24,16},{32,24},{40,32},{48,40},{56,48},{64,56},{72,6... | collective-permute-start | bytes 24584 | tf_op jit(solution)/shard_map/ppermute | solution.py:20
  489.9 8.1 %collective-permute-start.4 = (bf16[1,32,128]{2,1,0:T(8,128)(2,1)S(1)}, bf16[1,32,128]{2,1,0:T(8,128)(2,1)S(1)}, u32[]{:S(2)}, u32[]{:S(2)}) collective-permute-start(bf16[1,32,128]{2,1,0:T(8,128)(2,1)S(1)} %get-tuple-element.26), channel_id=1, source_target_pairs={{0,8},{8,16},{16,24},{24,32},{32,40},{40,48},{48,56},{56,64},{64,7... | collective-permute-start | bytes 24584 | tf_op jit(solution)/shard_map/ppermute | solution.py:18
  497.2 0.8 copy-start.20
  498.1 7.0 %collective-permute-start.6 = (bf16[34,1,128]{2,1,0:T(2,128)(2,1)S(1)}, bf16[34,1,128]{2,1,0:T(2,128)(2,1)S(1)}, u32[]{:S(2)}, u32[]{:S(2)}) collective-permute-start(bf16[34,1,128]{2,1,0:T(2,128)(2,1)S(1)} %get-tuple-element.17), channel_id=1, source_target_pairs={{1,0},{2,1},{3,2},{4,3},{5,4},{6,5},{7,6},{9,8},{10,9},{11,10},{12... | collective-permute-start | bytes 26120 | tf_op jit(solution)/shard_map/ppermute | solution.py:20
  501.4 4.3 collective-permute-start.7
  506.1 139.5 %copy-start.1 = (bf16[1,512,3]{1,2,0:T(4,128)(2,1)S(1)}, bf16[1,512,3]{1,2,0:T(4,128)(2,1)}, u32[]{:S(2)}) copy-start(bf16[1,512,3]{1,2,0:T(4,128)(2,1)} %param.18) | copy-start | bytes 9220
Sparse Core Ops, SparseCore 0:
  498.1 145.4 all-reduce.2
where the time goes:
time: 655 us; the launch traced here: 652 us
  waiting for transfers between devices  282 us (43%)
  local copies, waits for them, and re-layouts  199 us (30%)
  other arithmetic  73.1 us (11%)
  starting transfers between devices  52.3 us (8%)
  matrix products  31.7 us (5%)
  between operations  15 us (2%)
    psum x1, waiting for transfers between devices, local(): grad_conv = lax.psum(local_taps, ('ra', 'dec'))  135 us
    gather x1, local copies, waits for them, and re-layouts, local(): activation[row_index, col_index].reshape(object_count, crop_size)  108 us
    all_to_all x1, waiting for transfers between devices, local(): lax.all_to_all(send_rows.reshape(owners_all, capacity, crop_size), ('ra',...  76 us
    all_to_all x1, waiting for transfers between devices, local(): lax.all_to_all(crop_grad.reshape(owners_all, capacity, crop_size), ('ra',...  67.3 us
    unnamed x4, other arithmetic  56.2 us
    gather x2, local copies, waits for them, and re-layouts, local(): jnp.take(crop_rows, slot_safe, axis=0)  17.2 us
    ppermute x4, starting transfers between devices, padded_2(): lax.ppermute(tail, axis, [(i, (i + 1) % count) for i in range(ends)])  15.1 us
    gather x2, local copies, waits for them, and re-layouts, local(): back_rows = jnp.take(returned.reshape(-1, crop_size), slot_index, axis=0)  14.1 us
  transfers between devices with their start and end apart: 12, of which 6 were waited for; matrix products, arithmetic and copies ran while one was open for 25% of the time, Pallas kernels for 0%

commit v1 on v0

--- a/solution.py
+++ b/solution.py
@@ -172,7 +172,7 @@
                 preferred_element_type=jnp.float32,
             )
     local_taps = jnp.stack(tap_list).reshape(3, 3, channels, channels)
-    grad_conv = lax.psum(local_taps, ("ra", "dec"))
+    grad_conv = jnp.sum(lax.all_gather(local_taps, ("ra", "dec")), axis=0)
     grad_features = grad_feat.reshape(tile_rows, tile_cols, channels).astype(jnp.bfloat16)
     return (grad_features, grad_conv, grad_one[None])
 

time: 655 us -> 718 us (1.096)
  waiting for transfers between devices: 282 us -> 307 us
  other arithmetic: 73.1 us -> 97.1 us
  starting transfers between devices: 52.3 us -> 63.3 us
    all_gather x0 -> x1, waiting for transfers between devices: none -> 153 us  [local(): grad_conv = jnp.sum(lax.all_gather(local_taps, ('ra', 'dec')), axis=0)]
    psum x1 -> x0, waiting for transfers between devices: 135 us -> none  [local(): grad_conv = lax.psum(local_taps, ('ra', 'dec'))]
    reduce_sum x0 -> x1, other arithmetic: none -> 24.1 us  [local(): grad_conv = jnp.sum(lax.all_gather(local_taps, ('ra', 'dec')), axis=0)]
    all_to_all x1, starting transfers between devices: 11.1 us -> 21.6 us  [local(): lax.all_to_all(send_rows.reshape(owners_all, capacity, crop_size), ('ra',...]
    all_to_all x1, waiting for transfers between devices: 67.3 us -> 75.2 us  [local(): lax.all_to_all(crop_grad.reshape(owners_all, capacity, crop_size), ('ra',...]
  transfers between devices with their start and end apart: 12 -> 12, of which waited for: 6 -> 6; matrix products, arithmetic and copies ran while one was open for 25% -> 22% of each run, Pallas kernels for 0% -> 0%
where the time goes in v1:
time: 718 us; the launch traced here: 712 us
  waiting for transfers between devices  307 us (43%)
  local copies, waits for them, and re-layouts  197 us (27%)
  other arithmetic  97.1 us (14%)
  starting transfers between devices  63.3 us (9%)
  matrix products  32.7 us (5%)
  between operations  15.2 us (2%)
    all_gather x1, waiting for transfers between devices, local(): grad_conv = jnp.sum(lax.all_gather(local_taps, ('ra', 'dec')), axis=0)  153 us
    gather x1, local copies, waits for them, and re-layouts, local(): activation[row_index, col_index].reshape(object_count, crop_size)  108 us
    all_to_all x1, waiting for transfers between devices, local(): lax.all_to_all(send_rows.reshape(owners_all, capacity, crop_size), ('ra',...  76 us
    all_to_all x1, waiting for transfers between devices, local(): lax.all_to_all(crop_grad.reshape(owners_all, capacity, crop_size), ('ra',...  75.2 us
    unnamed x4, other arithmetic  56.2 us
    reduce_sum x1, other arithmetic, local(): grad_conv = jnp.sum(lax.all_gather(local_taps, ('ra', 'dec')), axis=0)  24.1 us
    all_to_all x1, starting transfers between devices, local(): lax.all_to_all(send_rows.reshape(owners_all, capacity, crop_size), ('ra',...  21.6 us
    gather x2, local copies, waits for them, and re-layouts, local(): jnp.take(crop_rows, slot_safe, axis=0)  17.2 us
  transfers between devices with their start and end apart: 12, of which 6 were waited for; matrix products, arithmetic and copies ran while one was open for 22% of the time, Pallas kernels for 0%

profile of v1, /device:TPU:1, one launch (start us, length us, event | category | flops | bytes accessed | tf_op | source)
XLA Modules:
  0.0 712.1 jit_solution(11535418767573319517)
XLA Ops:
  7.2 0.8 iota_compare_fusion.1
  8.3 0.9 fusion.48
  9.1 0.7 compare_select_fusion.2
  9.8 1.2 scatter_custom_fusion
  11.1 0.8 fusion.49
  11.9 1.4 gather_fusion
  13.4 0.3 gather.22
  14.2 0.8 copy.30
  14.9 11.5 %all-to-all-start = ((bf16[128,3,3]{1,2,0:T(4,128)(2,1)}), bf16[128,3,3]{1,2,0:T(4,128)(2,1)S(1)}, u32[]{:S(2)}, u32[]{:S(2)}) async-start(bf16[128,3,3]{1,2,0:T(4,128)(2,1)} %copy.30), calls=%async_computation | async-start | bytes 262144 | tf_op jit(solution)/shard_map/all_to_all | solution.py:120
  26.4 0.7 fusion.106
  27.2 3.3 collective-permute-start
  30.5 1.3 collective-permute-start.1
  31.8 0.8 fusion.107
  32.8 0.3 broadcast_or_fusion
  33.1 0.4 reshape.287
  33.6 1.1 constant_dynamic-update-slice_fusion.3
  34.7 0.5 collective-permute-done.1
  35.2 4.5 collective-permute-start.2
  39.7 2.3 collective-permute-start.3
  42.5 2.2 collective-permute-done.3
  44.7 0.3 pad_maximum_fusion.4
  46.9 107.8 %gather_fusion.1 = bf16[9800,128]{1,0:T(8,128)(2,1)} fusion(bf16[32,32,128]{2,1,0:T(8,128)(2,1)S(1)} %multiply_convert_fusion.4, s32[9800]{0:T(1024)S(1)} %reshape.287), kind=kCustom, calls=%fused_computation.1 | custom fusion | bytes 5096000 | tf_op jit(solution)/shard_map/gather | solution.py:91
  154.6 4.5 reshape.260
  159.2 5.8 gather_fusion.2
  165.0 11.5 %gather.25 = bf16[128,3,6272]{2,1,0:T(4,128)(2,1)} reshape(bf16[384,6272]{1,0:T(8,128)(2,1)} %gather_fusion.2) | data formatting | bytes 9633792 | tf_op jit(solution)/shard_map/jit(_take)/gather | solution.py:103
  176.4 9.0 %select_select_fusion = bf16[128,3,6272]{2,1,0:T(4,128)(2,1)} fusion(bf16[128,3,6272]{2,1,0:T(4,128)(2,1)} %gather.25, pred[128,3]{1,0:T(8,128)(4,1)S(1)} %broadcast_in_dim.103, pred[128,3]{1,0:T(8,128)(4,1)S(1)} %broadcast_in_dim.101), kind=kLoop, calls=%fused_computation.12 | loop fusion | flops 4816896 | bytes 9634560 | tf_op jit(solution)/shard_map/jit(_where)/select_n | solution.py:102
  185.4 21.6 %all-to-all-start.1 = ((bf16[128,3,6272]{2,1,0:T(4,128)(2,1)}), bf16[128,3,6272]{2,1,0:T(4,128)(2,1)}, u32[]{:S(2)}, u32[]{:S(2)}) async-start(bf16[128,3,6272]{2,1,0:T(4,128)(2,1)} %select_select_fusion), calls=%async_computation.1 | async-start | bytes 12845056 | tf_op jit(solution)/shard_map/all_to_all | solution.py:113
  207.7 76.0 %all-to-all-done.1 = bf16[128,3,6272]{2,1,0:T(4,128)(2,1)} async-done(((bf16[128,3,6272]{2,1,0:T(4,128)(2,1)}), bf16[128,3,6272]{2,1,0:T(4,128)(2,1)}, u32[]{:S(2)}, u32[]{:S(2)}) %all-to-all-start.1) | async-done | bytes 4816928 | tf_op jit(solution)/shard_map/all_to_all | solution.py:113
  283.6 12.5 %reshape.261 = bf16[384,6272]{1,0:T(8,128)(2,1)} reshape(bf16[128,3,6272]{2,1,0:T(4,128)(2,1)} %all-to-all-done.1) | data formatting | bytes 9633792 | tf_op jit(solution)/shard_map/reshape | solution.py:129
  296.1 6.3 fusion.4
  302.5 0.8 fusion.7
  303.3 8.9 %convolution_convert_fusion.1 = bf16[384,6272]{1,0:T(8,128)(2,1)} fusion(bf16[384,512]{1,0:T(8,128)(2,1)S(1)} %fusion.7, bf16[1,6272,512]{2,1,0:T(8,128)(2,1)} %param.16), kind=kOutput, calls=%fused_computation.7 | convolution fusion | flops 2468659200 | bytes 11632640 | tf_op jit(solution)/shard_map/dot_general | solution.py:54
  312.2 11.5 %reshape.262 = bf16[128,3,6272]{2,1,0:T(4,128)(2,1)} reshape(bf16[384,6272]{1,0:T(8,128)(2,1)} %convolution_convert_fusion.1) | data formatting | bytes 9633792 | tf_op jit(solution)/shard_map/reshape | solution.py:137
  323.7 6.4 all-to-all-start.2
  330.2 0.2 and_reduce_fusion
  330.7 0.4 copy.26
  331.0 0.4 reshape.317
  331.5 75.2 %all-to-all-done.2 = bf16[128,3,6272]{2,1,0:T(4,128)(2,1)} async-done(((bf16[128,3,6272]{2,1,0:T(4,128)(2,1)}), bf16[128,3,6272]{2,1,0:T(4,128)(2,1)}, u32[]{:S(2)}, u32[]{:S(2)}) %all-to-all-start.2) | async-done | bytes 4816928 | tf_op jit(solution)/shard_map/all_to_all | solution.py:136
  406.7 12.4 %reshape.263 = bf16[384,6272]{1,0:T(8,128)(2,1)} reshape(bf16[128,3,6272]{2,1,0:T(4,128)(2,1)} %all-to-all-done.2) | data formatting | bytes 9633792 | tf_op jit(solution)/shard_map/reshape | solution.py:143
  419.1 8.9 %gather_fusion.3 = bf16[200,6272]{1,0:T(8,128)(2,1)} fusion(bf16[384,6272]{1,0:T(8,128)(2,1)} %reshape.263, s32[1024]{0:T(1024)S(1)} %pad_clamp_fusion), kind=kCustom, calls=%fused_computation.3 | custom fusion | bytes 5018400 | tf_op jit(solution)/shard_map/jit(_take)/gather | solution.py:143
  428.0 5.2 gather.27
  433.2 3.0 select_convert_fusion
  436.2 6.7 reshape.319
  442.9 55.7 %scatter_custom_fusion.1 = f32[1024,128]{1,0:T(8,128)S(1)} fusion(s32[9800]{0:T(1024)S(1)} %reshape.317, f32[9800,128]{1,0:T(8,128)} %reshape.319, f32[]{:T(128)} %constant.27.clone.1), kind=kCustom, calls=%fused_computation.90 | custom fusion | flops 1254400 | bytes 524800
  498.9 0.3 fusion.21
  499.1 1.2 fusion.14
  500.4 0.3 fusion.20
  500.6 0.3 fusion.19
  500.9 0.3 fusion.18
  501.2 0.3 fusion.17
  501.5 0.3 fusion.16
  501.8 0.3 fusion.13
  502.1 0.3 fusion.15
  502.4 0.8 copy-done.20
  503.2 1.3 collective-permute-start.5
  504.5 4.1 collective-permute-start.4
  508.6 8.7 %fusion = bf16[1,6272,512]{2,1,0:T(8,128)(2,1)} fusion(bf16[384,6272]{1,0:T(8,128)(2,1)} %reshape.261, bf16[384,512]{1,0:T(8,128)(2,1)} %copy-done.27), kind=kOutput, calls=%fused_computation.8 | convolution fusion | flops 2469462016 | bytes 11632640 | tf_op jit(solution)/shard_map/dot_general | solution.py:51
  517.4 3.6 collective-permute-start.6
  521.0 3.5 collective-permute-start.7
  524.8 0.6 collective-permute-done.7
  526.0 0.2 convolution_add_fusion.6
  527.4 0.9 fusion.12
  528.4 152.6 %all-gather.2.cloned.1.call-done = f32[128,3,3,128,128]{4,3,2,1,0:T(8,128)} async-done(((f32[1,3,3,128,128]{4,3,2,1,0:T(8,128)}), f32[128,3,3,128,128]{4,3,2,1,0:T(8,128)}) %all-gather.2.cloned.1.call-update) | async-done | bytes 75497488 | tf_op jit(solution)/shard_map/all_gather | solution.py:175
  681.0 24.1 %reduce_sum.29 = f32[3,3,128,128]{3,2,1,0:T(8,128)} reduce(f32[128,3,3,128,128]{4,3,2,1,0:T(8,128)} %all-gather.2.cloned.1.call-done, f32[]{:T(128)} %constant.27.clone.1), dimensions={0}, to_apply=%region_6.7 | reduce | flops 18726912 | bytes 76087296 | tf_op jit(solution)/shard_map/reduce_sum | solution.py:175
  (122 shorter events, 6.6 us)
Async XLA Ops:
  7.2 295.3 %copy-start = (bf16[1,512,3]{1,2,0:T(4,128)(2,1)S(1)}, bf16[1,512,3]{1,2,0:T(4,128)(2,1)}, u32[]{:S(2)}) copy-start(bf16[1,512,3]{1,2,0:T(4,128)(2,1)} %param.18) | copy-start | bytes 9220
  7.2 34.9 %copy-start.4 = (bf16[3,3,128,128]{3,2,1,0:T(8,128)(2,1)S(1)}, bf16[3,3,128,128]{3,2,1,0:T(8,128)(2,1)}, u32[]{:S(2)}) copy-start(bf16[3,3,128,128]{3,2,1,0:T(8,128)(2,1)} %param.11) | copy-start | bytes 884740
  14.9 170.5 %all-to-all-start = ((bf16[128,3,3]{1,2,0:T(4,128)(2,1)}), bf16[128,3,3]{1,2,0:T(4,128)(2,1)S(1)}, u32[]{:S(2)}, u32[]{:S(2)}) async-start(bf16[128,3,3]{1,2,0:T(4,128)(2,1)} %copy.30), calls=%async_computation | async-start | bytes 262144 | tf_op jit(solution)/shard_map/all_to_all | solution.py:120
  27.2 6.4 collective-permute-start
  30.5 4.7 collective-permute-start.1
  33.1 12.9 %copy-start.2 = (bf16[32,32,128]{2,1,0:T(8,128)(2,1)S(1)}, bf16[32,32,128]{2,1,0:T(8,128)(2,1)}, u32[]{:S(2)}) copy-start(bf16[32,32,128]{2,1,0:T(8,128)(2,1)} %param.10) | copy-start | bytes 786436
  34.7 7.8 %copy-start.21 = (bf16[33,32,128]{2,1,0:T(8,128)(2,1)}, bf16[33,32,128]{2,1,0:T(8,128)(2,1)S(1)}, u32[]{:S(2)}) copy-start(bf16[33,32,128]{2,1,0:T(8,128)(2,1)S(1)} %get-tuple-element.28) | copy-start | bytes 811012
  35.2 6.9 copy-start.18
  35.2 7.3 %collective-permute-start.2 = (bf16[34,1,128]{2,1,0:T(2,128)(2,1)S(1)}, bf16[34,1,128]{2,1,0:T(2,128)(2,1)S(1)}, u32[]{:S(2)}, u32[]{:S(2)}) collective-permute-start(bf16[34,1,128]{2,1,0:T(2,128)(2,1)S(1)} %get-tuple-element.22), channel_id=1, source_target_pairs={{0,1},{1,2},{2,3},{3,4},{4,5},{5,6},{6,7},{8,9},{9,10},{10,11},{11... | collective-permute-start | bytes 26120 | tf_op jit(solution)/shard_map/ppermute | solution.py:18
  39.7 5.1 collective-permute-start.3
  42.0 4.5 copy-start.24
  45.1 1.1 copy-start.6
  45.1 1.6 copy-start.12
  45.1 1.6 copy-start.14
  45.1 1.6 copy-start.16
  45.1 1.7 copy-start.8
  45.1 1.7 copy-start.10
  185.4 98.2 %all-to-all-start.1 = ((bf16[128,3,6272]{2,1,0:T(4,128)(2,1)}), bf16[128,3,6272]{2,1,0:T(4,128)(2,1)}, u32[]{:S(2)}, u32[]{:S(2)}) async-start(bf16[128,3,6272]{2,1,0:T(4,128)(2,1)} %select_select_fusion), calls=%async_computation.1 | async-start | bytes 12845056 | tf_op jit(solution)/shard_map/all_to_all | solution.py:113
  207.2 88.9 %copy-start.25 = (f32[1,512]{1,0:T(1,128)S(1)}, f32[1,512]{1,0:T(1,128)}, u32[]{:S(2)}) copy-start(f32[1,512]{1,0:T(1,128)} %param.17) | copy-start | bytes 6148
  296.1 6.4 copy-start.26
  303.3 8.9 %copy-start.27 = (bf16[384,512]{1,0:T(8,128)(2,1)}, bf16[384,512]{1,0:T(8,128)(2,1)S(1)}, u32[]{:S(2)}) copy-start(bf16[384,512]{1,0:T(8,128)(2,1)S(1)} %fusion.7) | copy-start | bytes 1179652
  323.7 6.8 copy-start.23
  323.7 7.8 %copy-start.22 = (s32[1,1,200,1]{2,3,1,0:T(1,128)S(1)}, s32[1,1,200,1]{2,3,1,0:T(1,128)}, u32[]{:S(2)}) copy-start(s32[1,1,200,1]{2,3,1,0:T(1,128)} %param.14) | copy-start | bytes 2404
  323.7 83.0 %all-to-all-start.2 = ((bf16[128,3,6272]{2,1,0:T(4,128)(2,1)}), bf16[128,3,6272]{2,1,0:T(4,128)(2,1)}, u32[]{:S(2)}, u32[]{:S(2)}) async-start(bf16[128,3,6272]{2,1,0:T(4,128)(2,1)} %reshape.262), calls=%async_computation.2 | async-start | bytes 12845056 | tf_op jit(solution)/shard_map/all_to_all | solution.py:136
  330.0 350.9 %all-gather.2.cloned.1.call-start = ((), (), s32[]{:S(2)}) async-start(), calls=%async_computation.3 | async-start | bytes 76087296 | tf_op jit(solution)/shard_map/all_gather | solution.py:175
  436.2 62.7 %copy-start.15 = (bf16[32,32,128]{2,1,0:T(8,128)(2,1)S(1)}, bf16[32,32,128]{2,1,0:T(8,128)(2,1)}, u32[]{:S(2)}) copy-start(bf16[32,32,128]{2,1,0:T(8,128)(2,1)} %copy-done.14) | copy-start | bytes 786436
  436.2 64.2 %copy-start.13 = (bf16[32,32,128]{2,1,0:T(8,128)(2,1)S(1)}, bf16[32,32,128]{2,1,0:T(8,128)(2,1)}, u32[]{:S(2)}) copy-start(bf16[32,32,128]{2,1,0:T(8,128)(2,1)} %copy-done.12) | copy-start | bytes 786436
  436.2 64.5 %copy-start.11 = (bf16[32,32,128]{2,1,0:T(8,128)(2,1)S(1)}, bf16[32,32,128]{2,1,0:T(8,128)(2,1)}, u32[]{:S(2)}) copy-start(bf16[32,32,128]{2,1,0:T(8,128)(2,1)} %copy-done.10) | copy-start | bytes 786436
  436.2 64.7 %copy-start.3 = (bf16[32,32,128]{2,1,0:T(8,128)(2,1)S(1)}, bf16[32,32,128]{2,1,0:T(8,128)(2,1)}, u32[]{:S(2)}) copy-start(bf16[32,32,128]{2,1,0:T(8,128)(2,1)} %param.10) | copy-start | bytes 786436
  442.9 58.3 %copy-start.9 = (bf16[32,32,128]{2,1,0:T(8,128)(2,1)S(1)}, bf16[32,32,128]{2,1,0:T(8,128)(2,1)}, u32[]{:S(2)}) copy-start(bf16[32,32,128]{2,1,0:T(8,128)(2,1)} %copy-done.8) | copy-start | bytes 786436
  442.9 58.6 %copy-start.17 = (bf16[32,32,128]{2,1,0:T(8,128)(2,1)S(1)}, bf16[32,32,128]{2,1,0:T(8,128)(2,1)}, u32[]{:S(2)}) copy-start(bf16[32,32,128]{2,1,0:T(8,128)(2,1)} %copy-done.16) | copy-start | bytes 786436
  442.9 59.2 %copy-start.7 = (bf16[32,32,128]{2,1,0:T(8,128)(2,1)S(1)}, bf16[32,32,128]{2,1,0:T(8,128)(2,1)}, u32[]{:S(2)}) copy-start(bf16[32,32,128]{2,1,0:T(8,128)(2,1)} %copy-done.6) | copy-start | bytes 786436
  498.6 3.2 copy-start.19
  502.3 0.8 copy-start.20
  503.2 14.2 %collective-permute-start.5 = (bf16[1,32,128]{2,1,0:T(8,128)(2,1)S(1)}, bf16[1,32,128]{2,1,0:T(8,128)(2,1)S(1)}, u32[]{:S(2)}, u32[]{:S(2)}) collective-permute-start(bf16[1,32,128]{2,1,0:T(8,128)(2,1)S(1)} %get-tuple-element.27), channel_id=1, source_target_pairs={{8,0},{16,8},{24,16},{32,24},{40,32},{48,40},{56,48},{64,56},{72,6... | collective-permute-start | bytes 24584 | tf_op jit(solution)/shard_map/ppermute | solution.py:20
  504.5 20.0 %copy-start.5 = (bf16[3,3,128,128]{3,2,1,0:T(8,128)(2,1)S(1)}, bf16[3,3,128,128]{3,2,1,0:T(8,128)(2,1)}, u32[]{:S(2)}) copy-start(bf16[3,3,128,128]{3,2,1,0:T(8,128)(2,1)} %param.11) | copy-start | bytes 884740
  504.5 12.9 %collective-permute-start.4 = (bf16[1,32,128]{2,1,0:T(8,128)(2,1)S(1)}, bf16[1,32,128]{2,1,0:T(8,128)(2,1)S(1)}, u32[]{:S(2)}, u32[]{:S(2)}) collective-permute-start(bf16[1,32,128]{2,1,0:T(8,128)(2,1)S(1)} %get-tuple-element.26), channel_id=1, source_target_pairs={{0,8},{8,16},{16,24},{24,32},{32,40},{40,48},{48,56},{56,64},{64,7... | collective-permute-start | bytes 24584 | tf_op jit(solution)/shard_map/ppermute | solution.py:18
  517.4 7.4 %collective-permute-start.6 = (bf16[34,1,128]{2,1,0:T(2,128)(2,1)S(1)}, bf16[34,1,128]{2,1,0:T(2,128)(2,1)S(1)}, u32[]{:S(2)}, u32[]{:S(2)}) collective-permute-start(bf16[34,1,128]{2,1,0:T(2,128)(2,1)S(1)} %get-tuple-element.17), channel_id=1, source_target_pairs={{1,0},{2,1},{3,2},{4,3},{5,4},{6,5},{7,6},{9,8},{10,9},{11,10},{12... | collective-permute-start | bytes 26120 | tf_op jit(solution)/shard_map/ppermute | solution.py:20
  521.0 4.4 collective-permute-start.7
  681.0 24.1 %copy-start.1 = (bf16[1,512,3]{1,2,0:T(4,128)(2,1)S(1)}, bf16[1,512,3]{1,2,0:T(4,128)(2,1)}, u32[]{:S(2)}) copy-start(bf16[1,512,3]{1,2,0:T(4,128)(2,1)} %param.18) | copy-start | bytes 9220
Sparse Core Ops, SparseCore 0:
  503.3 177.6 all-gather.1
